TPU v7x, 256 devices: a whole 4x4x8 slice. The times are simulated.
256 devices in a mesh: comp: 2 (over core), seq: 16 (over y_lo, z), tp: 8 (over y_hi, x).
Axes of the slice: x: 4, y: 4 (y_hi: 2, y_lo: 2; y = y_hi * 2 + y_lo), z: 8, core: 2. Of those that a mesh axis runs over, the one named last changes fastest.
Arguments:
- inputs: bfloat16 [2, 8, 2048, 3072], P('comp', None, ('seq', 'tp')), may hold values from -6 to 6
- modulation: float32 [2, 8, 3, 3072], P('comp'), may hold values from -4 to 4
- w_qkv: bfloat16 [2, 3072, 3, 3072], P('comp', None, None, 'tp'), may hold values from -0.108253175 to 0.108253175
- w_attn_out: bfloat16 [2, 3072, 3072], P('comp', 'tp'), may hold values from -0.109375 to 0.109375
- qk_gain: float32 [2, 2, 128], P('comp'), may hold values from 1 to 5
- final_mod: float32 [8, 2, 3072], replicated, may hold values from -4 to 4
- w_final: bfloat16 [3072, 64], replicated, may hold values from -0.109375 to 0.109375
- w_embed: bfloat16 [64, 3072], replicated, may hold values from -0.75 to 0.75
- latent: float32 [8, 64, 2048], P(None, None, ('seq', 'tp')), may hold values from -6 to 6
Outputs:
- handed: bfloat16 [2, 8, 2048, 3072], P('comp', None, ('seq', 'tp'))
- velocity: float32 [8, 64, 2048], P(None, None, ('seq', 'tp'))
- advanced: float32 [8, 64, 2048], P(None, None, ('seq', 'tp'))
All inputs are finite; a program needn't handle non-finite values.
Results may differ from a plain program's by a relative error of at most 0.011.
Values may be sent and summed in bfloat16 or wider, within the bound.
No kernel may reach another device: no remote copies, remote signals or barrier semaphores. Data moves between devices by JAX's collectives and lax.ppermute only.
A program may use at most 192 MiB of HBM per device.

v0:
```python
import jax
import jax.numpy as jnp
from jax import lax
from jax.sharding import PartitionSpec as P

step_size = 0.02
norm_eps = 1e-06


def broadcast(block, axis, owner):
    block = jnp.where(lax.axis_index(axis) == owner, block, jnp.zeros_like(block))
    return lax.psum(block, axis)


def shifted(block, axis, distance):
    devices = range(lax.axis_size(axis))
    route = [((i - distance) % len(devices), i) for i in devices]
    return lax.ppermute(block, axis, route)


def layer_norm(values):
    center = values - jnp.mean(values, -1, keepdims=True)
    return center * lax.rsqrt(jnp.mean(center * center, -1, keepdims=True) + norm_eps)


def rms_norm(values, norm_gain):
    return values * lax.rsqrt(jnp.mean(values * values, -1, keepdims=True) + norm_eps) * norm_gain


def body(inputs, modulation, w_qkv, w_attn_out, qk_gain, final_mod, w_final, w_embed, latent):
    head_dim = qk_gain.shape[2]
    x_rows = inputs[0]
    samples = x_rows.shape[0]
    mod_rows = modulation[0]
    x_float = x_rows.astype(jnp.float32)
    x_mod = (
        layer_norm(x_float) * (1.0 + mod_rows[:, 1, None, :]) + mod_rows[:, 0, None, :]
    ).astype(jnp.bfloat16)
    weights = w_qkv[0]
    local_width = weights.shape[2]
    heads_local = local_width // head_dim
    norm_gains = qk_gain[0]
    scaling = head_dim ** (-0.5)
    mixed_rows = jnp.einsum(
        "srd,dje->srje",
        lax.all_gather(x_mod, "tp", axis=1, tiled=True),
        weights,
        preferred_element_type=jnp.float32,
    )
    unpacked = mixed_rows.reshape(
        mixed_rows.shape[0], mixed_rows.shape[1], 3, heads_local, head_dim
    )
    project_queried = rms_norm(unpacked[:, :, 0], norm_gains[0])
    keyed_rows = rms_norm(unpacked[:, :, 1], norm_gains[1])
    projected = jnp.stack([project_queried, keyed_rows, unpacked[:, :, 2]], 2).astype(jnp.bfloat16)
    queried = projected[:, :, 0]
    query_count = queried.shape[1]
    pairs = projected[:, :, 1:]
    start_max = jnp.full((samples, query_count, heads_local), -1e30, jnp.float32)
    shard_piece = lax.all_gather(pairs, "seq", axis=1, tiled=True)
    run_max = start_max
    scores = (
        jnp.einsum(
            "sqhd,skhd->sqhk", queried, shard_piece[:, :, 0], preferred_element_type=jnp.float32
        )
        * scaling
    )
    new_max = jnp.maximum(run_max, jnp.max(scores, -1))
    weight = jnp.exp(scores - new_max[..., None])
    run_sum = jnp.sum(weight, -1)
    summed = jnp.einsum(
        "sqhk,skhd->sqhd",
        weight.astype(jnp.bfloat16),
        shard_piece[:, :, 1],
        preferred_element_type=jnp.float32,
    )
    run_acc = summed
    run_max, run_sum, run_acc = (new_max, run_sum, run_acc)
    attended = (
        (run_acc / run_sum[..., None])
        .astype(jnp.bfloat16)
        .reshape(samples, query_count, local_width)
    )
    partial_out = jnp.einsum(
        "sqe,ed->sqd", attended, w_attn_out[0], preferred_element_type=jnp.float32
    )
    branch = lax.psum_scatter(
        partial_out.astype(jnp.bfloat16), "tp", scatter_dimension=1, tiled=True
    ).astype(jnp.float32)
    output = (x_float + mod_rows[:, 2, None, :] * branch).astype(jnp.bfloat16)
    final_in = (
        layer_norm(output.astype(jnp.float32)) * (1.0 + final_mod[:, 1, None, :])
        + final_mod[:, 0, None, :]
    ).astype(jnp.bfloat16)
    velocity = jnp.einsum("srd,dc->scr", final_in, w_final, preferred_element_type=jnp.float32)
    advanced = latent + step_size * velocity
    last_comp = lax.axis_size("comp") - 1
    position = lax.axis_index("comp")
    shared = broadcast(
        jnp.stack([velocity, advanced]).astype(jnp.bfloat16), "comp", last_comp
    ).astype(jnp.float32)
    embedded = jnp.einsum(
        "scr,cd->srd", advanced.astype(jnp.bfloat16), w_embed, preferred_element_type=jnp.float32
    ).astype(jnp.bfloat16)
    sending = jnp.where(position == last_comp, embedded, output)
    handed = shifted(sending, "comp", 1)
    return (handed[None], shared[0], shared[1])


def solution(mesh):
    in_specs = (
        P("comp", None, ("seq", "tp"), None),
        P("comp", None, None, None),
        P("comp", None, None, "tp"),
        P("comp", "tp", None),
        P("comp", None, None),
        P(),
        P(),
        P(),
        P(None, None, ("seq", "tp")),
    )
    out_specs = (
        P("comp", None, ("seq", "tp"), None),
        P(None, None, ("seq", "tp")),
        P(None, None, ("seq", "tp")),
    )
    return jax.shard_map(body, mesh=mesh, in_specs=in_specs, out_specs=out_specs, check_vma=False)
```

profile of v0, /device:TPU:1, one launch (start us, length us, event | category | flops | bytes accessed | tf_op | source)
XLA Modules:
  0.0 560.2 jit_solution(11027929013083755858)
XLA Ops:
  7.2 0.0 copy-start
  7.2 0.0 copy-start.1
  7.2 0.0 all-gather.3.cloned.1.call-start
  7.2 1.2 slice_bitcast_fusion.7
  8.4 1.3 convert_reduce_fusion.1
  9.8 0.0 copy-done.1
  9.8 0.3 fusion.22
  10.1 1.3 fusion.25
  11.4 0.0 all-gather.3.cloned.1.call-update
  11.5 0.0 copy-start.5
  11.5 0.0 all-gather.5.cloned.1.call-start
  11.5 10.3 %copy.18 = bf16[1,3072,3,384]{1,3,2,0:T(8,128)(2,1)} copy(bf16[1,3072,3,384]{3,1,2,0:T(8,128)(2,1)} %param.11) | data formatting | bytes 14155776 | tf_op args[2]
  21.8 0.0 copy-done.5
  21.8 87.1 %all-gather.3.cloned.1.call-done = bf16[8,128,3072]{2,1,0:T(8,128)(2,1)} async-done(((bf16[8,16,3072]{2,1,0:T(8,128)(2,1)}), bf16[8,128,3072]{2,1,0:T(8,128)(2,1)}) %all-gather.3.cloned.1.call-update) | async-done | bytes 6291472 | tf_op jit(solution)/shard_map/all_gather | solution.py:46
  108.9 10.5 %fusion.8 = f32[8,128,3,3,128]{1,4,3,2,0:T(8,128)S(1)} fusion(bf16[3,3,128,3072,1]{3,2,1,0,4:T(8,128)(2,1)} %bitcast.110, bf16[8,128,3072]{2,1,0:T(8,128)(2,1)} %all-gather.3.cloned.1.call-done), kind=kOutput, calls=%fused_computation.11 | convolution fusion | flops 7247757312 | bytes 18087936 | tf_op jit(solution)/shard_map/srd,dje->srje/dot_general | solution.py:44
  119.4 0.0 copy-start.2
  119.4 0.4 multiply_reduce_fusion
  119.8 0.1 slice.102
  120.0 1.6 copy-done.2
  121.6 0.3 multiply_convert_fusion.1
  121.9 1.4 pad_maximum_fusion
  123.3 0.0 all-gather.5.cloned.1.call-update
  123.3 0.2 reduce-scatter.2.cloned.1.call-start
  123.6 264.5 %all-gather.5.cloned.1.call-done = bf16[8,2048,2,3,128]{1,4,3,2,0:T(8,128)(2,1)} async-done(((bf16[8,128,2,3,128]{1,4,3,2,0:T(8,128)(2,1)}), bf16[8,2048,2,3,128]{1,4,3,2,0:T(8,128)(2,1)}) %all-gather.5.cloned.1.call-update) | async-done | bytes 25165840 | tf_op jit(solution)/shard_map/all_gather | solution.py:60
  388.0 13.9 %bitcast_reduce_fusion = (f32[8,128,3]{1,2,0:T(4,128)S(1)}, f32[8,3,2048,128]{3,2,1,0:T(8,128)}) fusion(f32[8,128,3,3,128]{1,4,3,2,0:T(8,128)} %copy-done.2, f32[128]{0:T(128)S(1)} %get-tuple-element.14, f32[8,128,3]{1,2,0:T(4,128)S(1)} %add_rsqrt_fusion, bf16[8,2048,2,3,128]{1,4,3,2,0:T(8,128)(2,1)} %all-gather.5.cloned.1.call-done), kind=kOutput, calls=%fused_computation.1 | convolution fusion | flops 1624372224 | bytes 39346688 | tf_op jit(solution)/shard_map/sqhd,skhd->sqhk/dot_general | solution.py:63
  402.0 10.5 %fusion.1 = f32[8,128,3]{1,2,0:T(4,128)S(1)} fusion(f32[8,3,2048,128]{3,2,1,0:T(8,128)} %get-tuple-element.17, f32[8,128,3]{1,2,0:T(4,128)S(1)} %broadcast_maximum_fusion), kind=kLoop, calls=%fused_computation.3 | loop fusion | flops 18871296 | bytes 25190400 | tf_op jit(solution)/shard_map/reduce_sum | solution.py:70
  412.4 15.2 %fusion.27 = bf16[8,128,3,128]{1,3,2,0:T(8,128)(2,1)S(1)} fusion(f32[8,3,2048,128]{3,2,1,0:T(8,128)} %get-tuple-element.17, f32[8,128,3]{1,2,0:T(4,128)S(1)} %broadcast_maximum_fusion, bf16[8,2048,2,3,128]{1,4,3,2,0:T(8,128)(2,1)} %all-gather.5.cloned.1.call-done, f32[8,128,3]{1,2,0:T(4,128)S(1)} %fusion.1), kind=kOutput, calls=%fused_computation.39 | convolution fusion | flops 1630273536 | bytes 38559744 | tf_op jit(solution)/shard_map/sqhk,skhd->sqhd/dot_general | solution.py:71
  427.6 0.0 copy-done
  427.6 5.4 convolution_convert_fusion
  433.0 0.0 copy-start.4
  433.0 0.0 reduce-scatter.2.cloned.1.call-update
  433.1 0.9 copy-done.4
  433.9 0.2 fusion.43
  434.2 108.9 %reduce-scatter.2.cloned.1.call-done = bf16[8,16,3072]{2,1,0:T(8,128)(2,1)} async-done(((bf16[8,128,3072]{2,1,0:T(8,128)(2,1)}), bf16[8,16,3072]{2,1,0:T(8,128)(2,1)}) %reduce-scatter.2.cloned.1.call-update) | async-done | bytes 786448 | tf_op jit(solution)/shard_map/reduce_scatter | solution.py:87
  543.1 0.0 copy-start.6
  543.1 0.0 copy-start.7
  543.1 1.5 convert_reduce_fusion
  544.6 0.0 copy-start.3
  544.7 0.3 fusion.18
  545.0 0.0 copy-done.6
  545.0 0.0 copy-done.7
  545.0 0.5 fusion.40
  545.5 0.1 copy-done.3
  545.6 1.2 fusion.10
  546.9 1.6 collective-permute-start
  548.5 3.6 psum.7
  552.1 0.7 slice_bitcast_fusion.8
  552.8 0.0 collective-permute-done
  552.8 0.9 copy.37
  (11 shorter events, 0.1 us)
Async XLA Ops:
  7.2 420.4 %copy-start = (bf16[1,384,3072]{2,1,0:T(8,128)(2,1)S(1)}, bf16[1,384,3072]{2,1,0:T(8,128)(2,1)}, u32[]{:S(2)}) copy-start(bf16[1,384,3072]{2,1,0:T(8,128)(2,1)} %param.12) | copy-start | bytes 7077892
  7.2 2.6 copy-start.1
  7.2 101.7 %all-gather.3.cloned.1.call-start = ((), (), s32[]{:S(2)}) async-start(), calls=%async_computation.1 | async-start | bytes 7077888 | tf_op jit(solution)/shard_map/all_gather | solution.py:46
  11.5 10.3 %copy-start.5 = (f32[1,2,128]{2,1,0:T(2,128)S(1)}, f32[1,2,128]{2,1,0:T(2,128)}, u32[]{:S(2)}) copy-start(f32[1,2,128]{2,1,0:T(2,128)} %param.13) | copy-start | bytes 3076
  11.5 376.6 %all-gather.5.cloned.1.call-start = ((), (), s32[]{:S(2)}) async-start(), calls=%async_computation.2 | async-start | bytes 26738688 | tf_op jit(solution)/shard_map/all_gather | solution.py:60
  119.4 2.2 copy-start.2
  123.3 419.8 %reduce-scatter.2.cloned.1.call-start = ((), (), s32[]{:S(2)}) async-start(), calls=%async_computation.3 | async-start | bytes 7077888 | tf_op jit(solution)/shard_map/reduce_scatter | solution.py:87
  433.0 0.9 copy-start.4
  543.1 1.9 copy-start.6
  543.1 1.9 copy-start.7
  544.6 1.0 copy-start.3
  546.9 5.9 %collective-permute-start = (bf16[8,16,3072]{2,1,0:T(8,128)(2,1)}, bf16[8,16,3072]{2,1,0:T(8,128)(2,1)S(1)}, u32[]{:S(2)}, u32[]{:S(2)}) collective-permute-start(bf16[8,16,3072]{2,1,0:T(8,128)(2,1)} %fusion.10), channel_id=1, source_target_pairs={{128,0},{0,128},{129,1},{1,129},{130,2},{2,130},{131,3},{3,131},{1... | collective-permute-start | bytes 2359304 | tf_op jit(solution)/shard_map/ppermute | solution.py:18
Sparse Core Ops, SparseCore 0:
  11.6 97.2 all-gather.2
  123.4 264.5 all-gather.4
  433.2 109.8 reduce-scatter.1
where the time goes:
time: 561 us; the launch traced here: 560 us
  waiting for transfers between devices  461 us (82%)
  matrix products  46.8 us (8%)
  other arithmetic  18.7 us (3%)
  local copies, waits for them, and re-layouts  14.8 us (3%)
  between operations  13.9 us (2%)
    all_gather x1, waiting for transfers between devices, body(): shard_piece = lax.all_gather(pairs, 'seq', axis=1, tiled=True)  264 us
    reduce_scatter x1, waiting for transfers between devices, body(): lax.psum_scatter(partial_out.astype(jnp.bfloat16), 'tp', scatter_dimensio...  109 us
    all_gather x1, waiting for transfers between devices, body(): lax.all_gather(x_mod, 'tp', axis=1, tiled=True)  87.1 us
    dot_general x1, matrix products, body(): jnp.einsum('sqhk,skhd->sqhd', weight.astype(jnp.bfloat16), shard_piece[:,...  15.2 us
    dot_general x1, matrix products, body(): jnp.einsum('sqhd,skhd->sqhk', queried, shard_piece[:, :, 0], preferred_el...  13.9 us
    unnamed x18, local copies, waits for them, and re-layouts  13.8 us
  transfers between devices with their start and end apart: 4, of which 3 were waited for; matrix products, arithmetic and copies ran while one was open for 2% of the time, Pallas kernels for 0%

commit v1 on v0

--- a/solution.py
+++ b/solution.py
@@ -57,7 +57,9 @@
     query_count = queried.shape[1]
     pairs = projected[:, :, 1:]
     start_max = jnp.full((samples, query_count, heads_local), -1e30, jnp.float32)
-    shard_piece = lax.all_gather(pairs, "seq", axis=1, tiled=True)
+    shard_piece = jnp.concatenate(
+        lax.all_to_all(jnp.stack([pairs] * lax.axis_size("seq")), "seq", 0, 0), axis=1
+    )
     run_max = start_max
     scores = (
         jnp.einsum(

time: 561 us -> 870 us (1.55)
  blocking collectives: 3.59 us -> 552 us
  waiting for transfers between devices: 461 us -> 187 us
  local copies, waits for them, and re-layouts: 14.8 us -> 47.9 us
    all_to_all x0 -> x1, blocking collectives: none -> 548 us  [body(): lax.all_to_all(jnp.stack([pairs] * lax.axis_size('seq')), 'seq', 0, 0)]
    all_gather x1 -> x0, waiting for transfers between devices: 264 us -> none  [body(): shard_piece = lax.all_gather(pairs, 'seq', axis=1, tiled=True)]
    reshape x0 -> x1, local copies, waits for them, and re-layouts: none -> 23.2 us  [body(): jnp.concatenate(lax.all_to_all(jnp.stack([pairs] * lax.axis_size('seq')),...]
    another operation x0 -> x2, local copies, waits for them, and re-layouts: none -> 9.91 us  [the longest x1 7.31 us: body(): jnp.stack([pairs] * lax.axis_size('seq'))]
    reduce_scatter x1, waiting for transfers between devices: 109 us -> 100 us  [body(): lax.psum_scatter(partial_out.astype(jnp.bfloat16), 'tp', scatter_dimensio...]
  transfers between devices with their start and end apart: 4 -> 3, of which waited for: 3 -> 2; matrix products, arithmetic and copies ran while one was open for 2% -> 1% of each run, Pallas kernels for 0% -> 0%
where the time goes in v1:
time: 870 us
  blocking collectives  552 us (63%)
  waiting for transfers between devices  187 us (21%)
  matrix products  48.2 us (6%)
  local copies, waits for them, and re-layouts  47.9 us (6%)
  other arithmetic  18.6 us (2%)
  between operations  14.2 us (2%)
    all_to_all x1, blocking collectives, body(): lax.all_to_all(jnp.stack([pairs] * lax.axis_size('seq')), 'seq', 0, 0)  548 us
    reduce_scatter x1, waiting for transfers between devices, body(): lax.psum_scatter(partial_out.astype(jnp.bfloat16), 'tp', scatter_dimensio...  100 us
    all_gather x1, waiting for transfers between devices, body(): lax.all_gather(x_mod, 'tp', axis=1, tiled=True)  87.1 us
    reshape x1, local copies, waits for them, and re-layouts, body(): jnp.concatenate(lax.all_to_all(jnp.stack([pairs] * lax.axis_size('seq')),...  23.2 us
  transfers between devices with their start and end apart: 3, of which 2 were waited for; matrix products, arithmetic and copies ran while one was open for 1% of the time, Pallas kernels for 0%

profile of v1, /device:TPU:1, one launch (start us, length us, event | category | flops | bytes accessed | tf_op | source)
XLA Modules:
  0.0 869.6 jit_solution(3249893844396708251)
XLA Ops:
  7.2 0.0 copy-start
  7.2 0.0 copy-start.1
  7.2 0.0 all-gather.2.cloned.1.call-start
  7.2 1.2 slice_bitcast_fusion.7
  8.4 1.3 convert_reduce_fusion.1
  9.8 0.0 copy-done.1
  9.8 0.3 fusion.22
  10.1 1.3 fusion.25
  11.4 0.0 all-gather.2.cloned.1.call-update
  11.5 0.0 copy-start.5
  11.5 0.0 reduce-scatter.2.cloned.1.call-start
  11.5 10.3 %copy.27 = bf16[1,3072,3,384]{1,3,2,0:T(8,128)(2,1)} copy(bf16[1,3072,3,384]{3,1,2,0:T(8,128)(2,1)} %param.11) | data formatting | bytes 14155776 | tf_op args[2]
  21.8 0.0 copy-done.5
  21.8 87.1 %all-gather.2.cloned.1.call-done = bf16[8,128,3072]{2,1,0:T(8,128)(2,1)} async-done(((bf16[8,16,3072]{2,1,0:T(8,128)(2,1)}), bf16[8,128,3072]{2,1,0:T(8,128)(2,1)}) %all-gather.2.cloned.1.call-update) | async-done | bytes 6291472 | tf_op jit(solution)/shard_map/all_gather | solution.py:46
  108.9 10.5 %fusion.8 = f32[8,128,3,3,128]{1,4,3,2,0:T(8,128)S(1)} fusion(bf16[3,3,128,3072,1]{3,2,1,0,4:T(8,128)(2,1)} %bitcast.115, bf16[8,128,3072]{2,1,0:T(8,128)(2,1)} %all-gather.2.cloned.1.call-done), kind=kOutput, calls=%fused_computation.11 | convolution fusion | flops 7247757312 | bytes 18087936 | tf_op jit(solution)/shard_map/srd,dje->srje/dot_general | solution.py:44
  119.4 0.0 copy-start.2
  119.4 0.4 multiply_reduce_fusion
  119.8 0.1 slice.102
  120.0 1.6 copy-done.2
  121.6 0.3 multiply_convert_fusion.1
  121.9 1.3 pad_maximum_fusion
  123.2 2.6 copy.28
  125.8 7.3 stack.15
  133.1 548.3 %all_to_all.5 = bf16[16,8,128,2,3,128]{5,2,4,1,3,0:T(8,128)(2,1)} all-to-all(bf16[16,8,128,2,3,128]{5,2,4,1,3,0:T(8,128)(2,1)S(1)} %stack.15), channel_id=1, replica_groups=mesh['comp'=2,'seq'=16,'tp'=8] {'seq'}, dimensions={0} | all-to-all | bytes 50331648 | tf_op jit(solution)/shard_map/all_to_all | solution.py:61
  681.4 23.2 %copy.29 = bf16[8,16,128,2,3,128]{5,2,1,4,0,3:T(8,128)(2,1)} copy(bf16[8,16,128,2,3,128]{5,2,4,0,3,1:T(8,128)(2,1)} %bitcast.112) | data formatting | bytes 50331648 | tf_op jit(solution)/shard_map/reshape | solution.py:60
  704.6 13.3 %bitcast_reduce_fusion = (f32[8,128,3]{1,2,0:T(4,128)S(1)}, f32[8,3,2048,128]{3,2,1,0:T(8,128)}) fusion(f32[8,128,3,3,128]{1,4,3,2,0:T(8,128)} %copy-done.2, f32[128]{0:T(128)S(1)} %get-tuple-element.14, f32[8,128,3]{1,2,0:T(4,128)S(1)} %get-tuple-element.20, bf16[8,2048,2,3,128]{4,1,3,0,2:T(8,128)(2,1)} %bitcast.113), kind=kOutput, calls=%fused_computation.1 | convolution fusion | flops 1624372224 | bytes 39346688 | tf_op jit(solution)/shard_map/sqhd,skhd->sqhk/dot_general | solution.py:65
  718.0 10.5 %fusion.1 = f32[8,128,3]{1,2,0:T(4,128)S(1)} fusion(f32[8,3,2048,128]{3,2,1,0:T(8,128)} %get-tuple-element.17, f32[8,128,3]{1,2,0:T(4,128)S(1)} %broadcast_maximum_fusion), kind=kLoop, calls=%fused_computation.3 | loop fusion | flops 18871296 | bytes 25190400 | tf_op jit(solution)/shard_map/reduce_sum | solution.py:72
  728.4 16.2 %fusion.27 = bf16[8,128,3,128]{1,3,2,0:T(8,128)(2,1)} fusion(f32[8,3,2048,128]{3,2,1,0:T(8,128)} %get-tuple-element.17, f32[8,128,3]{1,2,0:T(4,128)S(1)} %broadcast_maximum_fusion, bf16[8,2048,2,3,128]{4,1,3,0,2:T(8,128)(2,1)} %bitcast.114, f32[8,128,3]{1,2,0:T(4,128)S(1)} %fusion.1), kind=kOutput, calls=%fused_computation.39 | convolution fusion | flops 1630273536 | bytes 38559744 | tf_op jit(solution)/shard_map/sqhk,skhd->sqhd/dot_general | solution.py:73
  744.6 0.0 copy-done
  744.6 6.5 convolution_convert_fusion
  751.1 0.0 copy-start.4
  751.1 0.0 reduce-scatter.2.cloned.1.call-update
  751.1 0.9 copy-done.4
  752.0 0.2 fusion.43
  752.2 100.0 %reduce-scatter.2.cloned.1.call-done = bf16[8,16,3072]{2,1,0:T(8,128)(2,1)} async-done(((bf16[8,128,3072]{2,1,0:T(8,128)(2,1)}), bf16[8,16,3072]{2,1,0:T(8,128)(2,1)}) %reduce-scatter.2.cloned.1.call-update) | async-done | bytes 786448 | tf_op jit(solution)/shard_map/reduce_scatter | solution.py:89
  852.3 0.0 copy-start.6
  852.3 0.0 copy-start.7
  852.3 1.5 convert_reduce_fusion
  853.8 0.0 copy-start.3
  853.8 0.3 fusion.18
  854.2 0.0 copy-done.6
  854.2 0.0 copy-done.7
  854.2 0.5 fusion.40
  854.7 0.1 copy-done.3
  854.8 1.2 fusion.10
  856.0 1.6 collective-permute-start
  857.6 3.6 psum.7
  861.3 0.7 slice_bitcast_fusion.8
  861.9 0.0 collective-permute-done
  861.9 0.9 copy.48
  (10 shorter events, 0.1 us)
Async XLA Ops:
  7.2 737.4 %copy-start = (bf16[1,384,3072]{2,1,0:T(8,128)(2,1)S(1)}, bf16[1,384,3072]{2,1,0:T(8,128)(2,1)}, u32[]{:S(2)}) copy-start(bf16[1,384,3072]{2,1,0:T(8,128)(2,1)} %param.12) | copy-start | bytes 7077892
  7.2 2.6 copy-start.1
  7.2 101.7 %all-gather.2.cloned.1.call-start = ((), (), s32[]{:S(2)}) async-start(), calls=%async_computation.2 | async-start | bytes 7077888 | tf_op jit(solution)/shard_map/all_gather | solution.py:46
  11.5 10.3 %copy-start.5 = (f32[1,2,128]{2,1,0:T(2,128)S(1)}, f32[1,2,128]{2,1,0:T(2,128)}, u32[]{:S(2)}) copy-start(f32[1,2,128]{2,1,0:T(2,128)} %param.13) | copy-start | bytes 3076
  11.5 840.8 %reduce-scatter.2.cloned.1.call-start = ((), (), s32[]{:S(2)}) async-start(), calls=%async_computation.3 | async-start | bytes 7077888 | tf_op jit(solution)/shard_map/reduce_scatter | solution.py:89
  119.4 2.2 copy-start.2
  751.1 0.9 copy-start.4
  852.3 1.9 copy-start.6
  852.3 1.9 copy-start.7
  853.8 1.0 copy-start.3
  856.0 5.9 collective-permute-start
Sparse Core Ops, SparseCore 0:
  11.6 97.2 all-gather.1
  751.2 100.9 reduce-scatter.1
